TPU v7x, 128 devices: a whole 4x4x4 slice. The times are simulated.
128 devices in a mesh: section: 4 (over x), sample: 8 (over z, y_lo), tensor: 4 (over y_hi, core).
Axes of the slice: x: 4, y: 4 (y_hi: 2, y_lo: 2; y = y_hi * 2 + y_lo), z: 4, core: 2. Of those that a mesh axis runs over, the one named last changes fastest.
Arguments:
- queries: bfloat16 [4, 1024, 8192], P('section', 'sample', 'tensor'), may hold values from -4.5 to 4.5
- suffix_keys: bfloat16 [4, 1024, 1024], P('section', 'sample', 'tensor'), may hold values from -4.5 to 4.5
- suffix_values: bfloat16 [4, 1024, 1024], P('section', 'sample', 'tensor'), may hold values from -4.5 to 4.5
- output_grad: bfloat16 [4, 1024, 8192], P('section', 'sample', 'tensor'), may hold values from -192 to 192
- prefix_keys: bfloat16 [4, 4096, 1024], P('section', ('sample', 'tensor')), may hold values from -4.5 to 4.5
- prefix_values: bfloat16 [4, 4096, 1024], P('section', ('sample', 'tensor')), may hold values from -4.5 to 4.5
- kv_weight: bfloat16 [4, 8192, 2, 1024], P('section', None, None, 'tensor'), may hold values from -0.0625 to 0.0625
- prefix_states: bfloat16 [4, 4096, 8192], P('section', ('sample', 'tensor')), may hold values from -6 to 6
- norm_gain: bfloat16 [4, 8192], P('section'), may hold values from 0.099609375 to 1.8984375
- segment_ids: int32 [8, 128], P('sample'), may hold values from 0 to 1, never falling along the last dimension, each value on 1 to 96 neighbouring positions
- segment_prompt: int32 [8, 2], P('sample'), may hold values from 0 to 2
- block_table: int32 [3, 16], replicated, may hold values from 0 to 31, as said below
Outputs:
- query_grad: bfloat16 [4, 1024, 8192], P('section', 'sample', 'tensor')
- rollout_key_gradient: bfloat16 [4, 1024, 1024], P('section', 'sample', 'tensor')
- suffix_value_grad: bfloat16 [4, 1024, 1024], P('section', 'sample', 'tensor')
- prefix_key_grad: float32 [4, 4096, 1024], P('section', ('sample', 'tensor'))
- prefix_value_grad: float32 [4, 4096, 1024], P('section', ('sample', 'tensor'))
- prefix_state_gradient: float32 [4, 4096, 8192], P('section', ('sample', 'tensor'))
Inputs may be any that keep to these rules, and one draw needn't show every extreme that they name: `block_table`: each row lists 16 distinct pages; its first 8 entries are the same pages in every row, and every page of the pool appears in some row.
All inputs are finite; a program needn't handle non-finite values.
Results may differ from a plain program's by a relative error of at most 0.024.
Values may be sent and summed in bfloat16 or wider, within the bound.
No kernel may reach another device: no remote copies, remote signals or barrier semaphores. Data moves between devices by JAX's collectives and lax.ppermute only.
A program may use at most 192 MiB of HBM per device.

v0:
```python
import jax
import jax.numpy as jnp
from jax import lax
from jax.sharding import PartitionSpec as P

HEAD_SIZE = 128
PAGE = 128
MASKED_SCORE = -1e30
EPSILON = 1e-05


def entering(value, axis, join, neutral):
    count = lax.axis_size(axis)
    place = lax.axis_index(axis)
    ahead = count - 1 - place
    gathered = lax.all_gather(value.astype(jnp.bfloat16), axis)
    state = jnp.zeros_like(value) + jnp.asarray(neutral, value.dtype)

    def one(turn, state):
        source = count - 1 - turn
        return join(state, lax.dynamic_index_in_dim(gathered, source, 0, False).astype(value.dtype))

    return lax.fori_loop(0, ahead, one, state)


def visible_keys(seg_row, prompt_row, table, pooled_rows):
    tok_count = seg_row.shape[0]
    seg_hot = seg_row[:, None] == jnp.arange(prompt_row.shape[0], dtype=jnp.int32)[None, :]
    prompt_tok = jnp.sum(jnp.where(seg_hot, prompt_row[None, :], 0), axis=1)
    page_ids = jnp.arange(pooled_rows // PAGE, dtype=jnp.int32)
    member = jnp.any(table[:, :, None] == page_ids[None, None, :], axis=1)
    prompt_hot = prompt_tok[:, None] == jnp.arange(table.shape[0], dtype=jnp.int32)[None, :]
    member_tok = jnp.any(prompt_hot[:, :, None] & member[None, :, :], axis=1)
    prefix_seen = jnp.repeat(member_tok, PAGE, axis=1)
    position = jnp.arange(tok_count, dtype=jnp.int32)
    suffix_seen = (seg_row[:, None] == seg_row[None, :]) & (position[None, :] <= position[:, None])
    return jnp.concatenate([prefix_seen, suffix_seen], axis=1)


def attend_group(query_grp, grad_grp, key_rows, value_rows, visible):
    inv_root = query_grp.shape[-1] ** (-0.5)
    scores = (
        jnp.einsum("rgd,kd->rgk", query_grp, key_rows, preferred_element_type=jnp.float32)
        * inv_root
    )
    scores = jnp.where(visible[:, None, :], scores, MASKED_SCORE)
    row_max = jnp.max(scores, axis=2, keepdims=True)
    exponent = jnp.exp(scores - row_max)
    softmax_w = exponent / jnp.sum(exponent, axis=2, keepdims=True)
    weights_low = softmax_w.astype(jnp.bfloat16)
    attended = jnp.einsum(
        "rgk,kd->rgd", weights_low, value_rows, preferred_element_type=jnp.float32
    )
    delta_row = jnp.sum(grad_grp.astype(jnp.float32) * attended, axis=2, keepdims=True)
    weight_grad = jnp.einsum(
        "rgd,kd->rgk", grad_grp, value_rows, preferred_element_type=jnp.float32
    )
    score_grad = (softmax_w * (weight_grad - delta_row)).astype(jnp.bfloat16)
    query_out = (
        jnp.einsum("rgk,kd->rgd", score_grad, key_rows, preferred_element_type=jnp.float32)
        * inv_root
    )
    key_result = (
        jnp.einsum("rgk,rgd->kd", score_grad, query_grp, preferred_element_type=jnp.float32)
        * inv_root
    )
    value_out = jnp.einsum("rgk,rgd->kd", weights_low, grad_grp, preferred_element_type=jnp.float32)
    return (query_out, key_result, value_out)


def add_terms(earlier, later_term):
    return earlier + later_term


def on_device(
    queries,
    suffix_keys,
    suffix_values,
    output_grad,
    prefix_keys,
    prefix_values,
    kv_weight,
    prefix_states,
    norm_gain,
    segment_ids,
    segment_prompt,
    block_table,
):
    head_width = suffix_keys.shape[2]
    key_store, value_store = (
        lax.all_gather(prefix_keys, ("sample", "tensor"), axis=1, tiled=True),
        lax.all_gather(prefix_values, ("sample", "tensor"), axis=1, tiled=True),
    )
    offset = lax.axis_index("tensor") * head_width
    key_pool = lax.dynamic_slice_in_dim(key_store, offset, head_width, 2)[0]
    value_pool = lax.dynamic_slice_in_dim(value_store, offset, head_width, 2)[0]
    pooled_rows = key_pool.shape[0]
    tok_count = queries.shape[1]
    kv_local = head_width // HEAD_SIZE
    group_size = queries.shape[2] // head_width
    visible = visible_keys(segment_ids[0], segment_prompt[0], block_table, pooled_rows)
    query_rows = queries[0].reshape(tok_count, kv_local, group_size, HEAD_SIZE)
    grad_rows = output_grad[0].reshape(tok_count, kv_local, group_size, HEAD_SIZE)
    own_keys = suffix_keys[0]
    own_values = suffix_values[0]
    query_pieces, suffix_key_pieces, suffix_value_pieces, prefix_key_pieces, prefix_value_pieces = (
        [],
        [],
        [],
        [],
        [],
    )
    for head_index in range(kv_local):
        low_col = head_index * HEAD_SIZE
        key_rows = jnp.concatenate(
            [
                key_pool[:, low_col : low_col + HEAD_SIZE],
                own_keys[:, low_col : low_col + HEAD_SIZE],
            ],
            axis=0,
        )
        value_rows = jnp.concatenate(
            [
                value_pool[:, low_col : low_col + HEAD_SIZE],
                own_values[:, low_col : low_col + HEAD_SIZE],
            ],
            axis=0,
        )
        query_out, key_result, value_out = attend_group(
            query_rows[:, head_index], grad_rows[:, head_index], key_rows, value_rows, visible
        )
        query_pieces.append(query_out)
        prefix_key_pieces.append(key_result[:pooled_rows])
        suffix_key_pieces.append(key_result[pooled_rows:])
        prefix_value_pieces.append(value_out[:pooled_rows])
        suffix_value_pieces.append(value_out[pooled_rows:])
    query_grad = jnp.stack(query_pieces, axis=1).reshape(tok_count, -1).astype(jnp.bfloat16)
    rollout_key_gradient = jnp.concatenate(suffix_key_pieces, axis=1).astype(jnp.bfloat16)
    suffix_value_grad = jnp.concatenate(suffix_value_pieces, axis=1).astype(jnp.bfloat16)
    pooled_key = jnp.concatenate(prefix_key_pieces, axis=1)
    pooled_value = jnp.concatenate(prefix_value_pieces, axis=1)
    key_reduced, value_reduced = (
        lax.psum_scatter(
            pooled_key.astype(jnp.bfloat16), "sample", scatter_dimension=0, tiled=True
        ).astype(jnp.float32),
        lax.psum_scatter(
            pooled_value.astype(jnp.bfloat16), "sample", scatter_dimension=0, tiled=True
        ).astype(jnp.float32),
    )
    key_home, value_home = (
        lax.all_to_all(
            key_reduced.astype(jnp.bfloat16), "tensor", split_axis=0, concat_axis=1, tiled=True
        ).astype(key_reduced.dtype),
        lax.all_to_all(
            value_reduced.astype(jnp.bfloat16), "tensor", split_axis=0, concat_axis=1, tiled=True
        ).astype(value_reduced.dtype),
    )
    stacked = jnp.stack(
        [key_reduced.astype(jnp.bfloat16), value_reduced.astype(jnp.bfloat16)], axis=1
    )
    weight_local = kv_weight[0]
    normed_grad = lax.psum_scatter(
        lax.dot_general(
            stacked, weight_local, (((1, 2), (1, 2)), ((), ())), preferred_element_type=jnp.float32
        ).astype(jnp.bfloat16),
        "tensor",
        scatter_dimension=0,
        tiled=True,
    ).astype(jnp.float32)
    states = prefix_states[0].astype(jnp.float32)
    gain_wide = norm_gain[0].astype(jnp.float32)[None, :]
    inv_rms = lax.rsqrt(jnp.mean(states * states, axis=1, keepdims=True) + EPSILON)
    gained = gain_wide * normed_grad
    layer_term = inv_rms * gained - states * inv_rms**3 * jnp.mean(
        states * gained, axis=1, keepdims=True
    )
    higher_terms = entering(layer_term, "section", add_terms, jnp.zeros_like(layer_term))
    prefix_state_gradient = higher_terms + layer_term
    return (
        query_grad[None],
        rollout_key_gradient[None],
        suffix_value_grad[None],
        key_home[None],
        value_home[None],
        prefix_state_gradient[None],
    )


def solution(mesh):
    placed = (
        P("section", "sample", "tensor"),
        P("section", "sample", "tensor"),
        P("section", "sample", "tensor"),
        P("section", "sample", "tensor"),
        P("section", ("sample", "tensor"), None),
        P("section", ("sample", "tensor"), None),
        P("section", None, None, "tensor"),
        P("section", ("sample", "tensor"), None),
        P("section", None),
        P("sample", None),
        P("sample", None),
        P(),
    )
    return jax.shard_map(
        on_device,
        mesh=mesh,
        in_specs=placed,
        out_specs=(
            P("section", "sample", "tensor"),
            P("section", "sample", "tensor"),
            P("section", "sample", "tensor"),
            P("section", ("sample", "tensor"), None),
            P("section", ("sample", "tensor"), None),
            P("section", ("sample", "tensor"), None),
        ),
        check_vma=False,
    )
```

profile of v0, /device:TPU:1, one launch (start us, length us, event | category | flops | bytes accessed | tf_op | source)
XLA Modules:
  0.0 552.3 jit_solution(3952926247144493262)
XLA Ops:
  13.8 65.7 %all-gather.5.cloned.1.call-done = bf16[1,4096,1024]{2,1,0:T(8,128)(2,1)} async-done(((bf16[1,128,1024]{2,1,0:T(8,128)(2,1)}), bf16[1,4096,1024]{2,1,0:T(8,128)(2,1)}) %all-gather.5.cloned.1.call-update) | async-done | bytes 8388624 | tf_op jit(solution)/shard_map/all_gather | solution.py:91
  79.6 67.3 %all-gather.7.cloned.1.call-done = bf16[1,4096,1024]{2,1,0:T(8,128)(2,1)} async-done(((bf16[1,128,1024]{2,1,0:T(8,128)(2,1)}), bf16[1,4096,1024]{2,1,0:T(8,128)(2,1)}) %all-gather.7.cloned.1.call-update) | async-done | bytes 8388624 | tf_op jit(solution)/shard_map/all_gather | solution.py:92
  154.4 10.7 %fusion.67 = (f32[128,8]{0,1:T(8,128)S(1)}, f32[128,8,4224]{0,2,1:T(8,128)}) fusion(f32[4224,128,8]{1,0,2:T(8,128)S(1)} %fusion.33, pred[128,4224]{0,1:T(8,128)(4,1)S(1)} %pad_add_fusion), kind=kOutput, calls=%fused_computation.118 | output fusion | flops 17305728 | bytes 35147776 | tf_op jit(solution)/shard_map/sub | solution.py:48
  165.1 7.5 %fusion.13 = bf16[128,8,4224]{0,2,1:T(8,128)(2,1)S(1)} fusion(f32[128,8,4224]{0,2,1:T(8,128)} %get-tuple-element.112, f32[128,8]{0,1:T(8,128)S(1)} %get-tuple-element.111), kind=kLoop, calls=%fused_computation.23 | loop fusion | flops 8650752 | bytes 25956352 | tf_op jit(solution)/shard_map/convert_element_type | solution.py:50
  179.6 7.1 %fusion.3 = bf16[128,8,4224]{0,2,1:T(8,128)(2,1)} fusion(f32[128,8]{0,1:T(8,128)S(1)} %fusion.28, f32[128,8,4224]{0,2,1:T(8,128)S(1)} %bitcast.161, f32[128,8]{0,1:T(8,128)S(1)} %get-tuple-element.111, bf16[128,128]{1,0:T(8,128)(2,1)S(1)} %get-tuple-element.103, bf16[4096,128]{1,0:T(8,128)(2,1)} %get-tuple-element.97, bf16[128,2,8,128]{0,3,2,1:T(8,128)(2,1)} %bitcast.168), kind=kOutput, calls=%fused_computation.7 | convolution fusion | flops 1126760448 | bytes 27303936 | tf_op jit(solution)/shard_map/rgd,kd->rgk/dot_general | solution.py:55
  186.8 6.4 %fusion.17 = bf16[4224,128]{0,1:T(8,128)(2,1)S(1)} fusion(bf16[128,8,4224]{0,2,1:T(8,128)(2,1)} %fusion.3, bf16[128,2,8,128]{0,3,2,1:T(8,128)(2,1)} %bitcast.163), kind=kOutput, calls=%fused_computation.34 | convolution fusion | flops 1108377600 | bytes 9994240 | tf_op jit(solution)/shard_map/rgk,rgd->kd/dot_general | solution.py:64
  196.5 10.2 %fusion.66 = (f32[128,8]{0,1:T(8,128)S(1)}, f32[128,8,4224]{0,2,1:T(8,128)}) fusion(f32[4224,128,8]{1,0,2:T(8,128)S(1)} %fusion.32, pred[128,4224]{0,1:T(8,128)(4,1)S(1)} %pad_add_fusion), kind=kOutput, calls=%fused_computation.117 | output fusion | flops 17305728 | bytes 35147776 | tf_op jit(solution)/shard_map/sub | solution.py:48
  206.8 7.5 %fusion.14 = bf16[128,8,4224]{0,2,1:T(8,128)(2,1)S(1)} fusion(f32[128,8,4224]{0,2,1:T(8,128)} %get-tuple-element.110, f32[128,8]{0,1:T(8,128)S(1)} %get-tuple-element.109), kind=kLoop, calls=%fused_computation.24 | loop fusion | flops 8650752 | bytes 25956352 | tf_op jit(solution)/shard_map/convert_element_type | solution.py:50
  221.3 7.2 %fusion.2 = bf16[128,8,4224]{0,2,1:T(8,128)(2,1)} fusion(f32[128,8]{0,1:T(8,128)S(1)} %fusion.29, f32[128,8,4224]{0,2,1:T(8,128)S(1)} %bitcast.159, f32[128,8]{0,1:T(8,128)S(1)} %get-tuple-element.109, bf16[128,128]{1,0:T(8,128)(2,1)S(1)} %get-tuple-element.104, bf16[4096,128]{1,0:T(8,128)(2,1)} %get-tuple-element.98, bf16[128,2,8,128]{0,3,2,1:T(8,128)(2,1)} %bitcast.169), kind=kOutput, calls=%fused_computation.4 | convolution fusion | flops 1126760448 | bytes 27303936 | tf_op jit(solution)/shard_map/rgd,kd->rgk/dot_general | solution.py:55
  228.5 6.4 %fusion.18 = bf16[4224,128]{0,1:T(8,128)(2,1)S(1)} fusion(bf16[128,8,4224]{0,2,1:T(8,128)(2,1)} %fusion.2, bf16[128,2,8,128]{0,3,2,1:T(8,128)(2,1)S(1)} %bitcast.166), kind=kOutput, calls=%fused_computation.35 | convolution fusion | flops 1108377600 | bytes 9994240 | tf_op jit(solution)/shard_map/rgk,rgd->kd/dot_general | solution.py:64
  237.6 6.3 %fusion.19 = bf16[4224,128]{0,1:T(8,128)(2,1)S(1)} fusion(bf16[128,8,4224]{0,2,1:T(8,128)(2,1)} %copy-done.2, bf16[128,2,8,128]{0,3,2,1:T(8,128)(2,1)S(1)} %bitcast.170), kind=kOutput, calls=%fused_computation.36 | convolution fusion | flops 1107836928 | bytes 9994240 | tf_op jit(solution)/shard_map/rgk,rgd->kd/dot_general | solution.py:67
  245.1 6.4 %fusion.20 = bf16[4224,128]{0,1:T(8,128)(2,1)S(1)} fusion(bf16[128,8,4224]{0,2,1:T(8,128)(2,1)} %copy-done.3, bf16[128,2,8,128]{0,3,2,1:T(8,128)(2,1)S(1)} %bitcast.171), kind=kOutput, calls=%fused_computation.37 | convolution fusion | flops 1107836928 | bytes 9994240 | tf_op jit(solution)/shard_map/rgk,rgd->kd/dot_general | solution.py:67
  253.5 35.6 %reduce-scatter.4.cloned.1.call-done = bf16[512,256]{0,1:T(8,128)(2,1)} async-done(((bf16[4096,256]{0,1:T(8,128)(2,1)}), bf16[512,256]{0,1:T(8,128)(2,1)}) %reduce-scatter.4.cloned.1.call-update) | async-done | bytes 262160 | tf_op jit(solution)/shard_map/reduce_scatter | solution.py:143
  289.1 54.1 %reduce-scatter.6.cloned.1.call-done = bf16[512,256]{0,1:T(8,128)(2,1)} async-done(((bf16[4096,256]{0,1:T(8,128)(2,1)}), bf16[512,256]{0,1:T(8,128)(2,1)}) %reduce-scatter.6.cloned.1.call-update) | async-done | bytes 262160 | tf_op jit(solution)/shard_map/reduce_scatter | solution.py:146
  343.2 11.4 %bitcast_convert_fusion = bf16[512,8192]{1,0:T(8,128)(2,1)} fusion(bf16[8192,2,256]{2,1,0:T(2,128)(2,1)} %bitcast.185, bf16[512,1,256]{0,2,1:T(8,128)(2,1)} %bitcast.180, bf16[512,1,256]{0,2,1:T(8,128)(2,1)} %bitcast.179), kind=kOutput, calls=%fused_computation.11 | convolution fusion | flops 4299423744 | bytes 17301504 | tf_op jit(solution)/shard_map/dot_general | solution.py:163
  355.5 76.9 %reduce-scatter.8.cloned.1.call-done = bf16[128,8192]{1,0:T(8,128)(2,1)} async-done(((bf16[512,8192]{1,0:T(8,128)(2,1)}), bf16[128,8192]{1,0:T(8,128)(2,1)}) %reduce-scatter.8.cloned.1.call-update) | async-done | bytes 2097168 | tf_op jit(solution)/shard_map/reduce_scatter | solution.py:162
  438.1 5.1 fusion.31
  459.2 5.8 %all-to-all-done.1 = bf16[4,128,256]{1,2,0:T(8,128)(2,1)S(1)} async-done(((bf16[4,128,256]{1,2,0:T(8,128)(2,1)}), bf16[4,128,256]{1,2,0:T(8,128)(2,1)S(1)}, u32[]{:S(2)}, u32[]{:S(2)}) %all-to-all-start.1) | async-done | bytes 262176 | tf_op jit(solution)/shard_map/all_to_all | solution.py:154
  476.9 43.8 %all-gather.9.cloned.1.call-done = bf16[512,8192]{1,0:T(8,128)(2,1)} async-done(((bf16[128,8192]{1,0:T(8,128)(2,1)}), bf16[512,8192]{1,0:T(8,128)(2,1)}) %all-gather.9.cloned.1.call-update) | async-done | bytes 8388624 | tf_op jit(solution)/shard_map/all_gather | solution.py:16
  523.1 15.9 %while.12 = (s32[]{:T(128)}, f32[128,8192]{1,0:T(8,128)}, s32[]{:T(128)}, bf16[4,128,8192]{2,1,0:T(8,128)(2,1)}, s32[]{:T(128)}, /*index=5*/s32[]{:T(128)}, s32[]{:T(128)}, s32[]{:T(128)}) while((s32[]{:T(128)}, f32[128,8192]{1,0:T(8,128)}, s32[]{:T(128)}, bf16[4,128,8192]{2,1,0:T(8,128)(2,1)}, s32[]{:T(128)}, /*index=5*/s32[]{:T(128)}, ...), condition=%wide.region_15.16_spmd, body=%wide.region_14.15_spmd.sunk | while | flops 2097158 | bytes 10485903 | solution.py:23
  523.1 5.3 convert_add_fusion.2
  528.4 5.3 convert_add_fusion.2
  533.7 5.3 convert_add_fusion.2
  539.0 6.1 %add_bitcast_fusion = f32[1,128,8192]{2,1,0:T(8,128)} fusion(f32[128,8192]{1,0:T(8,128)} %get-tuple-element.62, bf16[128,8192]{1,0:T(8,128)(2,1)} %reduce-scatter.8.cloned.1.call-done, bf16[1,128,8192]{2,1,0:T(8,128)(2,1)S(1)} %copy-done, f32[128]{0:T(128)S(1)} %broadcast_multiply_fusion, f32[128]{0:T(128)S(1)} %get-tuple-element.108, ...), kind=kLoop, calls=%fused_computation.42 | loop fusion | flops 8388608 | bytes 12617216 | tf_op jit(solution)/shard_map/broadcast_in_dim | solution.py:185
  (140 shorter events, 73.9 us)
Async XLA Ops:
  7.2 72.3 %all-gather.5.cloned.1.call-start = ((), (), s32[]{:S(2)}) async-start(), calls=%async_computation.5 | async-start | bytes 8650752 | tf_op jit(solution)/shard_map/all_gather | solution.py:91
  8.0 138.9 %all-gather.7.cloned.1.call-start = ((), (), s32[]{:S(2)}) async-start(), calls=%async_computation.6 | async-start | bytes 8650752 | tf_op jit(solution)/shard_map/all_gather | solution.py:92
  8.7 280.4 %reduce-scatter.4.cloned.1.call-start = ((), (), s32[]{:S(2)}) async-start(), calls=%async_computation.7 | async-start | bytes 2359296 | tf_op jit(solution)/shard_map/reduce_scatter | solution.py:143
  12.1 137.2 %copy-start.9 = (bf16[1,128,2048]{1,2,0:T(8,128)(2,1)}, bf16[1,128,2048]{1,2,0:T(8,128)(2,1)S(1)}, u32[]{:S(2)}) copy-start(bf16[1,128,2048]{1,2,0:T(8,128)(2,1)S(1)} %copy.109) | copy-start | bytes 1572868
  13.6 137.4 %copy-start.18 = (bf16[128,128]{1,0:T(8,128)(2,1)}, bf16[128,128]{1,0:T(8,128)(2,1)S(1)}, u32[]{:S(2)}) copy-start(bf16[128,128]{1,0:T(8,128)(2,1)S(1)} %get-tuple-element.105) | copy-start | bytes 98308
  165.0 11.9 %copy-start.15 = (bf16[4096,128]{1,0:T(8,128)(2,1)S(1)}, bf16[4096,128]{1,0:T(8,128)(2,1)}, u32[]{:S(2)}) copy-start(bf16[4096,128]{1,0:T(8,128)(2,1)} %get-tuple-element.97) | copy-start | bytes 3145732
  165.0 11.9 %copy-start.17 = (bf16[128,1,8,128]{3,0,2,1:T(8,128)(2,1)S(1)}, bf16[128,1,8,128]{3,0,2,1:T(8,128)(2,1)}, u32[]{:S(2)}) copy-start(bf16[128,1,8,128]{3,0,2,1:T(8,128)(2,1)} %copy.164) | copy-start | bytes 786436
  165.0 14.4 %slice-start.5 = ((s8[17301504]{0:T(1024)(128)(4,1)}), s8[4194304]{0:T(1024)(128)(4,1)S(1)}, s32[]{:S(2)}) async-start(s8[17301504]{0:T(1024)(128)(4,1)} %bitcast.160), calls=%async_computation.16 | async-start | bytes 8388608
  165.0 14.4 %slice-start.6 = ((s8[17301504]{0:T(1024)(128)(4,1)}), s8[4194304]{0:T(1024)(128)(4,1)S(1)}, s32[]{:S(2)}) async-start(s8[17301504]{0:T(1024)(128)(4,1)} %bitcast.160), calls=%async_computation.17 | async-start | bytes 8388608
  165.0 14.4 %slice-start.7 = ((s8[17301504]{0:T(1024)(128)(4,1)}), s8[4194304]{0:T(1024)(128)(4,1)S(1)}, s32[]{:S(2)}) async-start(s8[17301504]{0:T(1024)(128)(4,1)} %bitcast.160), calls=%async_computation.18 | async-start | bytes 8388608
  165.1 14.4 %slice-start.8 = ((s8[17301504]{0:T(1024)(128)(4,1)}), s8[4194304]{0:T(1024)(128)(4,1)S(1)}, s32[]{:S(2)}) async-start(s8[17301504]{0:T(1024)(128)(4,1)} %bitcast.160), calls=%async_computation.19 | async-start | bytes 8388608
  206.7 11.9 %copy-start.14 = (bf16[4096,128]{1,0:T(8,128)(2,1)S(1)}, bf16[4096,128]{1,0:T(8,128)(2,1)}, u32[]{:S(2)}) copy-start(bf16[4096,128]{1,0:T(8,128)(2,1)} %get-tuple-element.98) | copy-start | bytes 3145732
  206.7 14.4 %slice-start = ((s8[17301504]{0:T(1024)(128)(4,1)}), s8[4194304]{0:T(1024)(128)(4,1)S(1)}, s32[]{:S(2)}) async-start(s8[17301504]{0:T(1024)(128)(4,1)} %bitcast.158), calls=%async_computation.11 | async-start | bytes 8388608
  206.7 14.4 %slice-start.1 = ((s8[17301504]{0:T(1024)(128)(4,1)}), s8[4194304]{0:T(1024)(128)(4,1)S(1)}, s32[]{:S(2)}) async-start(s8[17301504]{0:T(1024)(128)(4,1)} %bitcast.158), calls=%async_computation.12 | async-start | bytes 8388608
  206.7 14.4 %slice-start.2 = ((s8[17301504]{0:T(1024)(128)(4,1)}), s8[4194304]{0:T(1024)(128)(4,1)S(1)}, s32[]{:S(2)}) async-start(s8[17301504]{0:T(1024)(128)(4,1)} %bitcast.158), calls=%async_computation.13 | async-start | bytes 8388608
  206.7 14.4 %slice-start.3 = ((s8[17301504]{0:T(1024)(128)(4,1)}), s8[4194304]{0:T(1024)(128)(4,1)S(1)}, s32[]{:S(2)}) async-start(s8[17301504]{0:T(1024)(128)(4,1)} %bitcast.158), calls=%async_computation.14 | async-start | bytes 8388608
  228.5 7.5 %slice-start.10 = ((bf16[4224,128]{0,1:T(8,128)(2,1)}), bf16[4096,128]{0,1:T(8,128)(2,1)S(1)}, s32[]{:S(2)}) async-start(bf16[4224,128]{0,1:T(8,128)(2,1)} %copy-done.5), calls=%async_computation.21 | async-start | bytes 2097152 | tf_op jit(solution)/shard_map/slice | solution.py:133
  237.6 105.6 %reduce-scatter.6.cloned.1.call-start = ((), (), s32[]{:S(2)}) async-start(), calls=%async_computation.8 | async-start | bytes 2359296 | tf_op jit(solution)/shard_map/reduce_scatter | solution.py:146
  253.2 179.2 %reduce-scatter.8.cloned.1.call-start = ((), (), s32[]{:S(2)}) async-start(), calls=%async_computation.9 | async-start | bytes 10485760 | tf_op jit(solution)/shard_map/reduce_scatter | solution.py:162
  354.7 77.7 %copy-start = (bf16[1,128,8192]{2,1,0:T(8,128)(2,1)S(1)}, bf16[1,128,8192]{2,1,0:T(8,128)(2,1)}, u32[]{:S(2)}) copy-start(bf16[1,128,8192]{2,1,0:T(8,128)(2,1)} %param.21) | copy-start | bytes 6291460
  354.7 166.0 %all-gather.9.cloned.1.call-start = ((), (), s32[]{:S(2)}) async-start(), calls=%async_computation.10 | async-start | bytes 10485760 | tf_op jit(solution)/shard_map/all_gather | solution.py:16
  443.2 15.2 %copy-start.16 = (bf16[512,256]{0,1:T(8,128)(2,1)S(1)}, bf16[512,256]{0,1:T(8,128)(2,1)}, u32[]{:S(2)}) copy-start(bf16[512,256]{0,1:T(8,128)(2,1)} %reduce-scatter.4.cloned.1.call-done) | copy-start | bytes 786436
  454.1 10.9 %all-to-all-start.1 = ((bf16[4,128,256]{1,2,0:T(8,128)(2,1)}), bf16[4,128,256]{1,2,0:T(8,128)(2,1)S(1)}, u32[]{:S(2)}, u32[]{:S(2)}) async-start(bf16[4,128,256]{1,2,0:T(8,128)(2,1)} %copy_bitcast_fusion), calls=%async_computation.3 | async-start | bytes 524288 | tf_op jit(solution)/shard_map/all_to_all | solution.py:154
  465.0 10.9 %all-to-all-start = ((bf16[4,128,256]{1,2,0:T(8,128)(2,1)}), bf16[4,128,256]{1,2,0:T(8,128)(2,1)S(1)}, u32[]{:S(2)}, u32[]{:S(2)}) async-start(bf16[4,128,256]{1,2,0:T(8,128)(2,1)} %copy_bitcast_fusion.1), calls=%async_computation.1 | async-start | bytes 524288 | tf_op jit(solution)/shard_map/all_to_all | solution.py:151
  (21 other events, 76.2 us)
Sparse Core Ops, SparseCore 0:
  9.7 69.7 all-gather.4
  81.3 65.5 all-gather.6
  237.7 51.3 reduce-scatter.3
  291.4 51.8 reduce-scatter.5
  354.8 77.5 reduce-scatter.7
  438.2 82.4 all-gather.8
where the time goes:
time: 557 us; the launch traced here: 552 us
  waiting for transfers between devices  355 us (64%)
  matrix products  71.2 us (13%)
  other arithmetic  67.1 us (12%)
  local copies, waits for them, and re-layouts  35.1 us (6%)
  between operations  14.9 us (3%)
  starting transfers between devices  9.21 us (2%)
    reduce_scatter x1, waiting for transfers between devices, on_device(): lax.psum_scatter(lax.dot_general(stacked, weight_local, (((1, 2), (1, 2))...  76.9 us
    all_gather x1, waiting for transfers between devices, on_device(): lax.all_gather(prefix_values, ('sample', 'tensor'), axis=1, tiled=True)  67.3 us
    all_gather x1, waiting for transfers between devices, on_device(): lax.all_gather(prefix_keys, ('sample', 'tensor'), axis=1, tiled=True)  65.7 us
    reduce_scatter x1, waiting for transfers between devices, on_device(): lax.psum_scatter(pooled_value.astype(jnp.bfloat16), 'sample', scatter_dim...  54.1 us
    all_gather x1, waiting for transfers between devices, entering(): gathered = lax.all_gather(value.astype(jnp.bfloat16), axis)  43.8 us
    reduce_scatter x1, waiting for transfers between devices, on_device(): lax.psum_scatter(pooled_key.astype(jnp.bfloat16), 'sample', scatter_dimen...  35.6 us
    unnamed x81, local copies, waits for them, and re-layouts  22.6 us
    sub x2, other arithmetic, attend_group(): exponent = jnp.exp(scores - row_max)  20.9 us
  transfers between devices with their start and end apart: 8, of which 8 were waited for; matrix products, arithmetic and copies ran while one was open for 7% of the time, Pallas kernels for 0%

commit v1 on v0

--- a/solution.py
+++ b/solution.py
@@ -7,6 +7,13 @@
 PAGE = 128
 MASKED_SCORE = -1e30
 EPSILON = 1e-05
+
+
+def trade_parts(x, name, split, join):
+    size = lax.axis_size(name)
+    shards = jnp.stack(jnp.split(x, size, axis=split), axis=0)
+    shards = lax.all_to_all(shards, name, split_axis=0, concat_axis=0)
+    return jnp.concatenate(shards, axis=join)
 
 
 def entering(value, axis, join, neutral):
@@ -151,9 +158,7 @@
         lax.all_to_all(
             key_reduced.astype(jnp.bfloat16), "tensor", split_axis=0, concat_axis=1, tiled=True
         ).astype(key_reduced.dtype),
-        lax.all_to_all(
-            value_reduced.astype(jnp.bfloat16), "tensor", split_axis=0, concat_axis=1, tiled=True
-        ).astype(value_reduced.dtype),
+        trade_parts(value_reduced.astype(jnp.bfloat16), "tensor", 0, 1).astype(value_reduced.dtype),
     )
     stacked = jnp.stack(
         [key_reduced.astype(jnp.bfloat16), value_reduced.astype(jnp.bfloat16)], axis=1

time: 557 us -> 557 us (level)
  no operation moved by 1% of the time
where the time goes in v1:
time: 557 us; the launch traced here: 552 us
  waiting for transfers between devices  355 us (64%)
  matrix products  71.3 us (13%)
  other arithmetic  67.9 us (12%)
  local copies, waits for them, and re-layouts  34.4 us (6%)
  between operations  14.9 us (3%)
  starting transfers between devices  9.2 us (2%)
    reduce_scatter x1, waiting for transfers between devices, on_device(): lax.psum_scatter(lax.dot_general(stacked, weight_local, (((1, 2), (1, 2))...  76.9 us
    all_gather x1, waiting for transfers between devices, on_device(): lax.all_gather(prefix_values, ('sample', 'tensor'), axis=1, tiled=True)  67.3 us
    all_gather x1, waiting for transfers between devices, on_device(): lax.all_gather(prefix_keys, ('sample', 'tensor'), axis=1, tiled=True)  65.7 us
    reduce_scatter x1, waiting for transfers between devices, on_device(): lax.psum_scatter(pooled_value.astype(jnp.bfloat16), 'sample', scatter_dim...  54.1 us
    all_gather x1, waiting for transfers between devices, entering(): gathered = lax.all_gather(value.astype(jnp.bfloat16), axis)  44.7 us
    reduce_scatter x1, waiting for transfers between devices, on_device(): lax.psum_scatter(pooled_key.astype(jnp.bfloat16), 'sample', scatter_dimen...  35.5 us
    unnamed x81, local copies, waits for them, and re-layouts  22.6 us
    sub x2, other arithmetic, attend_group(): exponent = jnp.exp(scores - row_max)  20.8 us
  transfers between devices with their start and end apart: 8, of which 8 were waited for; matrix products, arithmetic and copies ran while one was open for 7% of the time, Pallas kernels for 0%

profile of v1, /device:TPU:1, one launch (start us, length us, event | category | flops | bytes accessed | tf_op | source)
XLA Modules:
  0.0 552.2 jit_solution(18222744860983658698)
XLA Ops:
  13.8 65.7 %all-gather.5.cloned.1.call-done = bf16[1,4096,1024]{2,1,0:T(8,128)(2,1)} async-done(((bf16[1,128,1024]{2,1,0:T(8,128)(2,1)}), bf16[1,4096,1024]{2,1,0:T(8,128)(2,1)}) %all-gather.5.cloned.1.call-update) | async-done | bytes 8388624 | tf_op jit(solution)/shard_map/all_gather | solution.py:98
  79.6 67.3 %all-gather.7.cloned.1.call-done = bf16[1,4096,1024]{2,1,0:T(8,128)(2,1)} async-done(((bf16[1,128,1024]{2,1,0:T(8,128)(2,1)}), bf16[1,4096,1024]{2,1,0:T(8,128)(2,1)}) %all-gather.7.cloned.1.call-update) | async-done | bytes 8388624 | tf_op jit(solution)/shard_map/all_gather | solution.py:99
  154.4 10.7 %fusion.67 = (f32[128,8]{0,1:T(8,128)S(1)}, f32[128,8,4224]{0,2,1:T(8,128)}) fusion(f32[4224,128,8]{1,0,2:T(8,128)S(1)} %fusion.33, pred[128,4224]{0,1:T(8,128)(4,1)S(1)} %pad_add_fusion), kind=kOutput, calls=%fused_computation.122 | output fusion | flops 17305728 | bytes 35147776 | tf_op jit(solution)/shard_map/sub | solution.py:55
  165.0 7.5 %fusion.13 = bf16[128,8,4224]{0,2,1:T(8,128)(2,1)S(1)} fusion(f32[128,8,4224]{0,2,1:T(8,128)} %get-tuple-element.116, f32[128,8]{0,1:T(8,128)S(1)} %get-tuple-element.115), kind=kLoop, calls=%fused_computation.23 | loop fusion | flops 8650752 | bytes 25956352 | tf_op jit(solution)/shard_map/convert_element_type | solution.py:57
  179.6 7.1 %fusion.3 = bf16[128,8,4224]{0,2,1:T(8,128)(2,1)} fusion(f32[128,8]{0,1:T(8,128)S(1)} %fusion.28, f32[128,8,4224]{0,2,1:T(8,128)S(1)} %bitcast.164, f32[128,8]{0,1:T(8,128)S(1)} %get-tuple-element.115, bf16[128,128]{1,0:T(8,128)(2,1)S(1)} %get-tuple-element.107, bf16[4096,128]{1,0:T(8,128)(2,1)} %get-tuple-element.97, bf16[128,2,8,128]{0,3,2,1:T(8,128)(2,1)} %bitcast.171), kind=kOutput, calls=%fused_computation.7 | convolution fusion | flops 1126760448 | bytes 27303936 | tf_op jit(solution)/shard_map/rgd,kd->rgk/dot_general | solution.py:62
  186.7 6.4 %fusion.17 = bf16[4224,128]{0,1:T(8,128)(2,1)S(1)} fusion(bf16[128,8,4224]{0,2,1:T(8,128)(2,1)} %fusion.3, bf16[128,2,8,128]{0,3,2,1:T(8,128)(2,1)} %bitcast.166), kind=kOutput, calls=%fused_computation.34 | convolution fusion | flops 1108377600 | bytes 9994240 | tf_op jit(solution)/shard_map/rgk,rgd->kd/dot_general | solution.py:71
  196.5 10.2 %fusion.66 = (f32[128,8]{0,1:T(8,128)S(1)}, f32[128,8,4224]{0,2,1:T(8,128)}) fusion(f32[4224,128,8]{1,0,2:T(8,128)S(1)} %fusion.32, pred[128,4224]{0,1:T(8,128)(4,1)S(1)} %pad_add_fusion), kind=kOutput, calls=%fused_computation.121 | output fusion | flops 17305728 | bytes 35147776 | tf_op jit(solution)/shard_map/sub | solution.py:55
  206.7 7.5 %fusion.14 = bf16[128,8,4224]{0,2,1:T(8,128)(2,1)S(1)} fusion(f32[128,8,4224]{0,2,1:T(8,128)} %get-tuple-element.114, f32[128,8]{0,1:T(8,128)S(1)} %get-tuple-element.113), kind=kLoop, calls=%fused_computation.24 | loop fusion | flops 8650752 | bytes 25956352 | tf_op jit(solution)/shard_map/convert_element_type | solution.py:57
  221.2 7.2 %fusion.2 = bf16[128,8,4224]{0,2,1:T(8,128)(2,1)} fusion(f32[128,8]{0,1:T(8,128)S(1)} %fusion.29, f32[128,8,4224]{0,2,1:T(8,128)S(1)} %bitcast.162, f32[128,8]{0,1:T(8,128)S(1)} %get-tuple-element.113, bf16[128,128]{1,0:T(8,128)(2,1)S(1)} %get-tuple-element.108, bf16[4096,128]{1,0:T(8,128)(2,1)} %get-tuple-element.98, bf16[128,2,8,128]{0,3,2,1:T(8,128)(2,1)} %bitcast.172), kind=kOutput, calls=%fused_computation.4 | convolution fusion | flops 1126760448 | bytes 27303936 | tf_op jit(solution)/shard_map/rgd,kd->rgk/dot_general | solution.py:62
  228.4 6.4 %fusion.18 = bf16[4224,128]{0,1:T(8,128)(2,1)S(1)} fusion(bf16[128,8,4224]{0,2,1:T(8,128)(2,1)} %fusion.2, bf16[128,2,8,128]{0,3,2,1:T(8,128)(2,1)S(1)} %bitcast.169), kind=kOutput, calls=%fused_computation.35 | convolution fusion | flops 1108377600 | bytes 9994240 | tf_op jit(solution)/shard_map/rgk,rgd->kd/dot_general | solution.py:71
  237.6 6.3 %fusion.19 = bf16[4224,128]{0,1:T(8,128)(2,1)S(1)} fusion(bf16[128,8,4224]{0,2,1:T(8,128)(2,1)} %copy-done.2, bf16[128,2,8,128]{0,3,2,1:T(8,128)(2,1)S(1)} %bitcast.173), kind=kOutput, calls=%fused_computation.36 | convolution fusion | flops 1107836928 | bytes 9994240 | tf_op jit(solution)/shard_map/rgk,rgd->kd/dot_general | solution.py:74
  245.1 6.4 %fusion.20 = bf16[4224,128]{0,1:T(8,128)(2,1)S(1)} fusion(bf16[128,8,4224]{0,2,1:T(8,128)(2,1)} %copy-done.3, bf16[128,2,8,128]{0,3,2,1:T(8,128)(2,1)S(1)} %bitcast.174), kind=kOutput, calls=%fused_computation.37 | convolution fusion | flops 1107836928 | bytes 9994240 | tf_op jit(solution)/shard_map/rgk,rgd->kd/dot_general | solution.py:74
  253.5 35.5 %reduce-scatter.4.cloned.1.call-done = bf16[512,256]{0,1:T(8,128)(2,1)} async-done(((bf16[4096,256]{0,1:T(8,128)(2,1)}), bf16[512,256]{0,1:T(8,128)(2,1)}) %reduce-scatter.4.cloned.1.call-update) | async-done | bytes 262160 | tf_op jit(solution)/shard_map/reduce_scatter | solution.py:150
  289.1 54.1 %reduce-scatter.6.cloned.1.call-done = bf16[512,256]{0,1:T(8,128)(2,1)} async-done(((bf16[4096,256]{0,1:T(8,128)(2,1)}), bf16[512,256]{0,1:T(8,128)(2,1)}) %reduce-scatter.6.cloned.1.call-update) | async-done | bytes 262160 | tf_op jit(solution)/shard_map/reduce_scatter | solution.py:153
  343.2 11.5 %bitcast_convert_fusion = bf16[512,8192]{1,0:T(8,128)(2,1)} fusion(bf16[8192,2,256]{2,1,0:T(2,128)(2,1)} %bitcast.188, bf16[512,1,256]{0,2,1:T(8,128)(2,1)} %bitcast.183, bf16[512,1,256]{0,2,1:T(8,128)(2,1)} %bitcast.182), kind=kOutput, calls=%fused_computation.11 | convolution fusion | flops 4299423744 | bytes 17301504 | tf_op jit(solution)/shard_map/dot_general | solution.py:168
  355.4 76.9 %reduce-scatter.8.cloned.1.call-done = bf16[128,8192]{1,0:T(8,128)(2,1)} async-done(((bf16[512,8192]{1,0:T(8,128)(2,1)}), bf16[128,8192]{1,0:T(8,128)(2,1)}) %reduce-scatter.8.cloned.1.call-update) | async-done | bytes 2097168 | tf_op jit(solution)/shard_map/reduce_scatter | solution.py:167
  438.1 5.1 fusion.31
  443.3 5.0 fusion.30
  476.0 44.7 %all-gather.9.cloned.1.call-done = bf16[512,8192]{1,0:T(8,128)(2,1)} async-done(((bf16[128,8192]{1,0:T(8,128)(2,1)}), bf16[512,8192]{1,0:T(8,128)(2,1)}) %all-gather.9.cloned.1.call-update) | async-done | bytes 8388624 | tf_op jit(solution)/shard_map/all_gather | solution.py:23
  523.1 15.9 %while.12 = (s32[]{:T(128)}, f32[128,8192]{1,0:T(8,128)}, s32[]{:T(128)}, bf16[4,128,8192]{2,1,0:T(8,128)(2,1)}, s32[]{:T(128)}, /*index=5*/s32[]{:T(128)}, s32[]{:T(128)}, s32[]{:T(128)}) while((s32[]{:T(128)}, f32[128,8192]{1,0:T(8,128)}, s32[]{:T(128)}, bf16[4,128,8192]{2,1,0:T(8,128)(2,1)}, s32[]{:T(128)}, /*index=5*/s32[]{:T(128)}, ...), condition=%wide.region_15.16_spmd, body=%wide.region_14.15_spmd.sunk | while | flops 2097158 | bytes 10485903 | solution.py:30
  523.1 5.3 convert_add_fusion.2
  528.4 5.3 convert_add_fusion.2
  533.7 5.3 convert_add_fusion.2
  539.0 6.1 %add_bitcast_fusion = f32[1,128,8192]{2,1,0:T(8,128)} fusion(f32[128,8192]{1,0:T(8,128)} %get-tuple-element.62, bf16[128,8192]{1,0:T(8,128)(2,1)} %reduce-scatter.8.cloned.1.call-done, bf16[1,128,8192]{2,1,0:T(8,128)(2,1)S(1)} %copy-done, f32[128]{0:T(128)S(1)} %broadcast_multiply_fusion, f32[128]{0:T(128)S(1)} %get-tuple-element.112, ...), kind=kLoop, calls=%fused_computation.42 | loop fusion | flops 8388608 | bytes 12617216 | tf_op jit(solution)/shard_map/broadcast_in_dim | solution.py:190
  (141 shorter events, 73.7 us)
Async XLA Ops:
  7.2 72.3 %all-gather.5.cloned.1.call-start = ((), (), s32[]{:S(2)}) async-start(), calls=%async_computation.5 | async-start | bytes 8650752 | tf_op jit(solution)/shard_map/all_gather | solution.py:98
  8.0 138.9 %all-gather.7.cloned.1.call-start = ((), (), s32[]{:S(2)}) async-start(), calls=%async_computation.6 | async-start | bytes 8650752 | tf_op jit(solution)/shard_map/all_gather | solution.py:99
  8.7 280.4 %reduce-scatter.4.cloned.1.call-start = ((), (), s32[]{:S(2)}) async-start(), calls=%async_computation.7 | async-start | bytes 2359296 | tf_op jit(solution)/shard_map/reduce_scatter | solution.py:150
  12.1 137.2 %copy-start.9 = (bf16[1,128,2048]{1,2,0:T(8,128)(2,1)}, bf16[1,128,2048]{1,2,0:T(8,128)(2,1)S(1)}, u32[]{:S(2)}) copy-start(bf16[1,128,2048]{1,2,0:T(8,128)(2,1)S(1)} %copy.108) | copy-start | bytes 1572868
  13.6 137.4 %copy-start.18 = (bf16[128,128]{1,0:T(8,128)(2,1)}, bf16[128,128]{1,0:T(8,128)(2,1)S(1)}, u32[]{:S(2)}) copy-start(bf16[128,128]{1,0:T(8,128)(2,1)S(1)} %get-tuple-element.109) | copy-start | bytes 98308
  165.0 11.9 %copy-start.15 = (bf16[4096,128]{1,0:T(8,128)(2,1)S(1)}, bf16[4096,128]{1,0:T(8,128)(2,1)}, u32[]{:S(2)}) copy-start(bf16[4096,128]{1,0:T(8,128)(2,1)} %get-tuple-element.97) | copy-start | bytes 3145732
  165.0 11.9 %copy-start.17 = (bf16[128,1,8,128]{3,0,2,1:T(8,128)(2,1)S(1)}, bf16[128,1,8,128]{3,0,2,1:T(8,128)(2,1)}, u32[]{:S(2)}) copy-start(bf16[128,1,8,128]{3,0,2,1:T(8,128)(2,1)} %copy.162) | copy-start | bytes 786436
  165.0 14.4 %slice-start.5 = ((s8[17301504]{0:T(1024)(128)(4,1)}), s8[4194304]{0:T(1024)(128)(4,1)S(1)}, s32[]{:S(2)}) async-start(s8[17301504]{0:T(1024)(128)(4,1)} %bitcast.163), calls=%async_computation.16 | async-start | bytes 8388608
  165.0 14.4 %slice-start.6 = ((s8[17301504]{0:T(1024)(128)(4,1)}), s8[4194304]{0:T(1024)(128)(4,1)S(1)}, s32[]{:S(2)}) async-start(s8[17301504]{0:T(1024)(128)(4,1)} %bitcast.163), calls=%async_computation.17 | async-start | bytes 8388608
  165.0 14.4 %slice-start.7 = ((s8[17301504]{0:T(1024)(128)(4,1)}), s8[4194304]{0:T(1024)(128)(4,1)S(1)}, s32[]{:S(2)}) async-start(s8[17301504]{0:T(1024)(128)(4,1)} %bitcast.163), calls=%async_computation.18 | async-start | bytes 8388608
  165.0 14.4 %slice-start.8 = ((s8[17301504]{0:T(1024)(128)(4,1)}), s8[4194304]{0:T(1024)(128)(4,1)S(1)}, s32[]{:S(2)}) async-start(s8[17301504]{0:T(1024)(128)(4,1)} %bitcast.163), calls=%async_computation.19 | async-start | bytes 8388608
  206.7 11.9 %copy-start.14 = (bf16[4096,128]{1,0:T(8,128)(2,1)S(1)}, bf16[4096,128]{1,0:T(8,128)(2,1)}, u32[]{:S(2)}) copy-start(bf16[4096,128]{1,0:T(8,128)(2,1)} %get-tuple-element.98) | copy-start | bytes 3145732
  206.7 14.4 %slice-start = ((s8[17301504]{0:T(1024)(128)(4,1)}), s8[4194304]{0:T(1024)(128)(4,1)S(1)}, s32[]{:S(2)}) async-start(s8[17301504]{0:T(1024)(128)(4,1)} %bitcast.161), calls=%async_computation.11 | async-start | bytes 8388608
  206.7 14.4 %slice-start.1 = ((s8[17301504]{0:T(1024)(128)(4,1)}), s8[4194304]{0:T(1024)(128)(4,1)S(1)}, s32[]{:S(2)}) async-start(s8[17301504]{0:T(1024)(128)(4,1)} %bitcast.161), calls=%async_computation.12 | async-start | bytes 8388608
  206.7 14.4 %slice-start.2 = ((s8[17301504]{0:T(1024)(128)(4,1)}), s8[4194304]{0:T(1024)(128)(4,1)S(1)}, s32[]{:S(2)}) async-start(s8[17301504]{0:T(1024)(128)(4,1)} %bitcast.161), calls=%async_computation.13 | async-start | bytes 8388608
  206.7 14.4 %slice-start.3 = ((s8[17301504]{0:T(1024)(128)(4,1)}), s8[4194304]{0:T(1024)(128)(4,1)S(1)}, s32[]{:S(2)}) async-start(s8[17301504]{0:T(1024)(128)(4,1)} %bitcast.161), calls=%async_computation.14 | async-start | bytes 8388608
  228.4 7.5 %slice-start.10 = ((bf16[4224,128]{0,1:T(8,128)(2,1)}), bf16[4096,128]{0,1:T(8,128)(2,1)S(1)}, s32[]{:S(2)}) async-start(bf16[4224,128]{0,1:T(8,128)(2,1)} %copy-done.5), calls=%async_computation.21 | async-start | bytes 2097152 | tf_op jit(solution)/shard_map/slice | solution.py:140
  237.5 105.6 %reduce-scatter.6.cloned.1.call-start = ((), (), s32[]{:S(2)}) async-start(), calls=%async_computation.8 | async-start | bytes 2359296 | tf_op jit(solution)/shard_map/reduce_scatter | solution.py:153
  253.2 179.1 %reduce-scatter.8.cloned.1.call-start = ((), (), s32[]{:S(2)}) async-start(), calls=%async_computation.9 | async-start | bytes 10485760 | tf_op jit(solution)/shard_map/reduce_scatter | solution.py:167
  354.6 77.7 %copy-start = (bf16[1,128,8192]{2,1,0:T(8,128)(2,1)S(1)}, bf16[1,128,8192]{2,1,0:T(8,128)(2,1)}, u32[]{:S(2)}) copy-start(bf16[1,128,8192]{2,1,0:T(8,128)(2,1)} %param.21) | copy-start | bytes 6291460
  354.7 166.0 %all-gather.9.cloned.1.call-start = ((), (), s32[]{:S(2)}) async-start(), calls=%async_computation.10 | async-start | bytes 10485760 | tf_op jit(solution)/shard_map/all_gather | solution.py:23
  443.2 9.1 %copy-start.16 = (bf16[512,256]{0,1:T(8,128)(2,1)S(1)}, bf16[512,256]{0,1:T(8,128)(2,1)}, u32[]{:S(2)}) copy-start(bf16[512,256]{0,1:T(8,128)(2,1)} %reduce-scatter.4.cloned.1.call-done) | copy-start | bytes 786436
  453.1 10.9 %all-to-all-start = ((bf16[4,128,256]{1,2,0:T(8,128)(2,1)}), bf16[4,128,256]{1,2,0:T(8,128)(2,1)S(1)}, u32[]{:S(2)}, u32[]{:S(2)}) async-start(bf16[4,128,256]{1,2,0:T(8,128)(2,1)} %copy_bitcast_fusion), calls=%async_computation.1 | async-start | bytes 524288 | tf_op jit(solution)/shard_map/all_to_all | solution.py:158
  464.0 10.9 %all-to-all-start.1 = ((bf16[4,128,256]{1,2,0:T(8,128)(2,1)}), bf16[4,128,256]{1,2,0:T(8,128)(2,1)S(1)}, u32[]{:S(2)}, u32[]{:S(2)}) async-start(bf16[4,128,256]{1,2,0:T(8,128)(2,1)} %pad_maximum_fusion.3), calls=%async_computation.3 | async-start | bytes 524288 | tf_op jit(solution)/shard_map/all_to_all | solution.py:15
  (21 other events, 76.2 us)
Sparse Core Ops, SparseCore 0:
  9.7 69.7 all-gather.4
  81.3 65.5 all-gather.6
  237.7 51.3 reduce-scatter.3
  291.3 51.8 reduce-scatter.5
  354.8 77.5 reduce-scatter.7
  438.2 82.4 all-gather.8
